TPU v7x, 512 devices: a whole 4x8x8 slice. The times are simulated.
512 devices in a mesh: sec: 4 (over x), lat: 8 (over z), lon: 16 (over y, core).
Axes of the slice: x: 4, y: 8, z: 8, core: 2. Of those that a mesh axis runs over, the one named last changes fastest.
Arguments:
- state: float32 [4, 75, 32, 2048], P('sec', None, 'lat', 'lon'), may hold values from -6 to 6
- mixing: bfloat16 [4, 75, 32, 2048], P('sec', None, 'lat', 'lon'), may hold values from 0.05 to 50
- eastward: bfloat16 [4, 75, 32, 2048], P('sec', None, 'lat', 'lon'), may hold values from -0.44921875 to 0.44921875
- northward: bfloat16 [4, 75, 32, 2048], P('sec', None, 'lat', 'lon'), may hold values from -0.44921875 to 0.44921875
- sea_mask: int32 [32, 2048], P('lat', 'lon'), may hold values 0 or 1
- weights: bfloat16 [4, 8, 16, 16, 16, 512], P('sec', 'lat', 'lon'), may hold values from -1.5 to 1.5
- source_block: int32 [4, 8, 16, 128, 4], P('sec', 'lat', 'lon'), may hold values from 0 to 31
- dest_block: int32 [4, 8, 16, 128, 4], P('sec', 'lat', 'lon'), may hold values from 0 to 31
- record_counts: int32 [4, 8, 16, 128], P('sec', 'lat', 'lon'), may hold values from 0 to 4, as said below
Outputs:
- adjoint: float32 [4, 75, 32, 2048], P('sec', None, 'lat', 'lon')
Inputs may be any that keep to these rules, and one draw needn't show every extreme that they name: `record_counts`: in every section some receiving device has 4 live slots from every sending device.
All inputs are finite; a program needn't handle non-finite values. No bound on the sum of `sea_mask` on one device may be relied on, other than what follows from the above.
Results may differ from a plain program's by a relative error of at most 0.0003.
Values sent between devices are 32-bit elements; how exact they have to be, the bound alone decides.
No kernel may reach another device: no remote copies, remote signals or barrier semaphores. Data moves between devices by JAX's collectives and lax.ppermute only.
A program may use at most 64 MiB of HBM per device.

v0:
```python
import jax
import jax.numpy as jnp
from jax import lax
from jax.sharding import PartitionSpec as P

NCPL = 4
NSUB = 2


def extended(block, sides, width, periodic):
    for axis, dim in sides:
        count = lax.axis_size(axis)
        forward = [(i, i + 1) for i in range(count - 1)]
        if periodic:
            forward.append((count - 1, 0))
        backward = [(target, source) for source, target in forward]
        low = lax.ppermute(
            lax.slice_in_dim(block, block.shape[dim] - width, None, axis=dim), axis, forward
        )
        high = lax.ppermute(lax.slice_in_dim(block, 0, width, axis=dim), axis, backward)
        block = jnp.concatenate([low, block, high], axis=dim)
    return block


def column_solve(right, coeff):
    zero_row = jnp.zeros_like(coeff[:1])
    lower_band = jnp.concatenate([zero_row, coeff[1:]], axis=0)
    upper_band = jnp.concatenate([coeff[1:], zero_row], axis=0)
    centre = 1.0 + lower_band + upper_band

    def sweep_down(carried, entries):
        prior_c, prior_z = carried
        centre_k, beneath, overhead, right_k = entries
        pivot_value = centre_k + beneath * prior_c
        factor = -overhead / pivot_value
        partial_value = (right_k + beneath * prior_z) / pivot_value
        return ((factor, partial_value), (factor, partial_value))

    start_pair = (jnp.zeros_like(right[0]), jnp.zeros_like(right[0]))
    _, (factors, partials) = lax.scan(
        sweep_down, start_pair, (centre, lower_band, upper_band, right)
    )

    def sweep_up(carried, entries):
        factor, partial_value = entries
        solved_k = partial_value - factor * carried
        return (solved_k, solved_k)

    _, solved = lax.scan(sweep_up, jnp.zeros_like(right[0]), (factors, partials), reverse=True)
    return solved


def advect(mixed_adj, east_speed, north_speed):
    east_flux = east_speed.astype(jnp.float32) * mixed_adj
    north_flux = north_speed.astype(jnp.float32) * mixed_adj
    east_rim = extended(east_flux, (("lon", 2),), 1, True)
    north_rim = extended(north_flux, (("lat", 1),), 1, False)
    east_diff = east_rim[:, :, 2:] - east_rim[:, :, :-2]
    north_diff = north_rim[:, 2:, :] - north_rim[:, :-2, :]
    return mixed_adj + 0.5 * (east_diff + north_diff)


def couple(field_part, weights, source_block, dest_block, record_counts, air_factor):
    block_cells = weights.shape[3]
    capacity = source_block.shape[-1]
    peer_count = record_counts.shape[-1]
    surface = field_part[-1].reshape(-1, block_cells)
    block_count = surface.shape[0]
    gathered = jnp.take(surface, source_block.reshape(-1), axis=0)
    weight_table = weights[0, 0, 0].astype(jnp.float32)
    contribution = jnp.einsum("diz,zi->dz", weight_table, gathered, precision=lax.Precision.HIGHEST)
    received = lax.all_to_all(
        contribution.reshape(block_cells, peer_count, capacity),
        ("lat", "lon"),
        split_axis=1,
        concat_axis=1,
        tiled=True,
    )
    arrived = received.reshape(block_cells, peer_count * capacity)
    live_slot = (
        jnp.arange(capacity, dtype=jnp.int32)[None, :] < record_counts[0, 0, 0][:, None]
    ).reshape(-1)
    matches = dest_block.reshape(-1)[:, None] == jnp.arange(block_count, dtype=jnp.int32)[None, :]
    one_hot = jnp.logical_and(matches, live_slot[:, None]).astype(jnp.float32)
    accumulated = jnp.dot(
        arrived, one_hot, precision=lax.Precision.HIGHEST, preferred_element_type=jnp.float32
    )
    summed = lax.psum(accumulated * air_factor, "sec")
    return summed.T.reshape(field_part.shape[1], field_part.shape[2])


def local(
    state, mixing, eastward, northward, sea_mask, weights, source_block, dest_block, record_counts
):
    section = lax.axis_index("sec")
    section_count = lax.axis_size("sec")
    is_ocean = section == section_count - 1
    air_factor = jnp.where(is_ocean, 0.0, 1.0).astype(jnp.float32)
    ocean_keep = sea_mask.astype(jnp.float32)
    keep_factor = jnp.where(is_ocean, ocean_keep, jnp.ones_like(ocean_keep))
    field_part = state[0]
    mix_part = mixing[0]
    east_part = eastward[0]
    north_part = northward[0]
    for coupling in range(NCPL):
        for repeat in range(NSUB):
            mixed_adj = column_solve(field_part, mix_part.astype(jnp.float32))
            field_part = advect(mixed_adj, east_part, north_part) * keep_factor
        forcing = couple(field_part, weights, source_block, dest_block, record_counts, air_factor)
        field_part = field_part.at[0].add(
            jnp.where(is_ocean, forcing * ocean_keep, jnp.zeros_like(forcing))
        )
    return field_part[None]


def solution(mesh):
    in_specs = (
        P("sec", None, "lat", "lon"),
        P("sec", None, "lat", "lon"),
        P("sec", None, "lat", "lon"),
        P("sec", None, "lat", "lon"),
        P("lat", "lon"),
        P("sec", "lat", "lon", None, None, None),
        P("sec", "lat", "lon", None, None),
        P("sec", "lat", "lon", None, None),
        P("sec", "lat", "lon", None),
    )
    out_specs = P("sec", None, "lat", "lon")
    return jax.shard_map(local, mesh=mesh, in_specs=in_specs, out_specs=out_specs, check_vma=False)
```

profile of v0, /device:TPU:2, one launch (start us, length us, event | category | flops | bytes accessed | tf_op | source)
XLA Modules:
  0.0 362.5 jit_solution(979839688588339115)
XLA Ops:
  1.1 52.6 %while.276 = (s32[]{:T(128)}, f32[4,128]{1,0:T(4,128)S(1)}, f32[4,128]{1,0:T(4,128)S(1)}, f32[75,4,128]{2,1,0:T(4,128)S(1)}, f32[75,4,128]{2,1,0:T(4,128)S(1)}, ...) while((s32[]{:T(128)}, f32[4,128]{1,0:T(4,128)S(1)}, ...), condition=%wide.region_1.2_spmd.clone, body=%wide.region_0.1_spmd.clone.sunk | while | flops 4611 | bytes 20603 | solution.py:40
  53.7 2.7 while.277
  57.6 2.9 collective-permute-start
  60.6 1.3 collective-permute-start.2
  61.9 4.9 %collective-permute-start.3 = (f32[75,1,128]{2,1,0:T(1,128)S(1)}, f32[75,1,128]{2,1,0:T(1,128)S(1)}, u32[]{:S(2)}, u32[]{:S(2)}) collective-permute-start(f32[75,1,128]{2,1,0:T(1,128)S(1)} %get-tuple-element.2005), channel_id=1, source_target_pairs={{0,16},{16,32},{32,48},{48,64},{64,80},{80,96},{96,112},{1,17},{17... | collective-permute-start | bytes 115208 | tf_op jit(solution)/shard_map/ppermute | solution.py:17
  68.9 3.2 while.278
  72.1 2.7 while.279
  75.8 2.1 collective-permute-start.4
  78.6 1.3 collective-permute-start.6
  79.8 4.9 %collective-permute-start.7 = (f32[75,1,128]{2,1,0:T(1,128)}, f32[75,1,128]{2,1,0:T(1,128)S(1)}, u32[]{:S(2)}, u32[]{:S(2)}) collective-permute-start(f32[75,1,128]{2,1,0:T(1,128)} %get-tuple-element.1999), channel_id=1, source_target_pairs={{0,16},{16,32},{32,48},{48,64},{64,80},{80,96},{96,112},{1,17},{17... | collective-permute-start | bytes 115208 | tf_op jit(solution)/shard_map/ppermute | solution.py:17
  84.8 2.1 copy.17
  86.9 1.3 fusion.73
  89.5 2.6 fusion.127
  92.1 16.9 %all-to-all-start = ((f32[16,128,4]{0,2,1:T(4,128)}), f32[16,128,4]{0,2,1:T(4,128)S(1)}, u32[]{:S(2)}, u32[]{:S(2)}) async-start(f32[16,128,4]{0,2,1:T(4,128)} %bitcast.13), calls=%async_computation | async-start | bytes 524288 | tf_op jit(solution)/shard_map/all_to_all | solution.py:72
  109.5 14.2 %all-to-all-done = f32[16,128,4]{0,2,1:T(4,128)S(1)} async-done(((f32[16,128,4]{0,2,1:T(4,128)}), f32[16,128,4]{0,2,1:T(4,128)S(1)}, u32[]{:S(2)}, u32[]{:S(2)}) %all-to-all-start) | async-done | bytes 32800 | tf_op jit(solution)/shard_map/all_to_all | solution.py:72
  124.4 8.6 %psum.28 = f32[4,128]{1,0:T(4,128)S(1)} all-reduce(f32[4,128]{1,0:T(4,128)S(1)} %reshape.204), channel_id=1, replica_groups=mesh['sec'=4,'lat'=8,'lon'=16] {'sec'}, use_global_device_ids=true, to_apply=%region_8.10 | all-reduce | flops 512 | bytes 4096 | tf_op jit(solution)/shard_map/psum | solution.py:88
  133.1 3.2 while.280
  136.4 2.7 while.281
  141.1 5.2 %collective-permute-start.11 = (f32[75,1,128]{2,1,0:T(1,128)}, f32[75,1,128]{2,1,0:T(1,128)}, u32[]{:S(2)}, u32[]{:S(2)}) collective-permute-start(f32[75,1,128]{2,1,0:T(1,128)} %get-tuple-element.1993), channel_id=1, source_target_pairs={{0,16},{16,32},{32,48},{48,64},{64,80},{80,96},{96,112},{1,17},{17... | collective-permute-start | bytes 115208 | tf_op jit(solution)/shard_map/ppermute | solution.py:17
  147.6 2.5 collective-permute-done.8
  150.2 3.0 collective-permute-done.9
  153.8 1.3 fusion.67
  155.2 3.0 while.282
  158.3 2.7 while.283
  161.2 1.3 collective-permute-start.14
  162.5 4.7 %collective-permute-start.15 = (f32[75,1,128]{2,1,0:T(1,128)S(1)}, f32[75,1,128]{2,1,0:T(1,128)S(1)}, u32[]{:S(2)}, u32[]{:S(2)}) collective-permute-start(f32[75,1,128]{2,1,0:T(1,128)S(1)} %get-tuple-element.1987), channel_id=1, source_target_pairs={{0,16},{16,32},{32,48},{48,64},{64,80},{80,96},{96,112},{1,17},{17... | collective-permute-start | bytes 115208 | tf_op jit(solution)/shard_map/ppermute | solution.py:17
  167.9 2.2 collective-permute-done.12
  170.1 3.1 collective-permute-done.13
  174.9 2.6 fusion.128
  177.5 7.4 %all-to-all-start.1 = ((f32[16,128,4]{0,2,1:T(4,128)}), f32[16,128,4]{0,2,1:T(4,128)S(1)}, u32[]{:S(2)}, u32[]{:S(2)}) async-start(f32[16,128,4]{0,2,1:T(4,128)} %bitcast.23), calls=%async_computation.1 | async-start | bytes 524288 | tf_op jit(solution)/shard_map/all_to_all | solution.py:72
  184.9 14.7 %all-to-all-done.1 = f32[16,128,4]{0,2,1:T(4,128)S(1)} async-done(((f32[16,128,4]{0,2,1:T(4,128)}), f32[16,128,4]{0,2,1:T(4,128)S(1)}, u32[]{:S(2)}, u32[]{:S(2)}) %all-to-all-start.1) | async-done | bytes 32800 | tf_op jit(solution)/shard_map/all_to_all | solution.py:72
  200.3 10.1 %psum.29 = f32[4,128]{1,0:T(4,128)S(1)} all-reduce(f32[4,128]{1,0:T(4,128)S(1)} %reshape.208), channel_id=1, replica_groups=mesh['sec'=4,'lat'=8,'lon'=16] {'sec'}, use_global_device_ids=true, to_apply=%region_17.19 | all-reduce | flops 512 | bytes 4096 | tf_op jit(solution)/shard_map/psum | solution.py:88
  210.5 3.2 while.284
  213.7 2.7 while.285
  218.5 5.2 %collective-permute-start.19 = (f32[75,1,128]{2,1,0:T(1,128)}, f32[75,1,128]{2,1,0:T(1,128)}, u32[]{:S(2)}, u32[]{:S(2)}) collective-permute-start(f32[75,1,128]{2,1,0:T(1,128)} %get-tuple-element.1981), channel_id=1, source_target_pairs={{0,16},{16,32},{32,48},{48,64},{64,80},{80,96},{96,112},{1,17},{17... | collective-permute-start | bytes 115208 | tf_op jit(solution)/shard_map/ppermute | solution.py:17
  225.0 2.5 collective-permute-done.16
  227.5 3.0 collective-permute-done.17
  231.2 1.3 fusion.55
  232.5 3.0 while.286
  235.6 2.7 while.287
  238.5 1.3 collective-permute-start.22
  239.8 4.5 %collective-permute-start.23 = (f32[75,1,128]{2,1,0:T(1,128)S(1)}, f32[75,1,128]{2,1,0:T(1,128)S(1)}, u32[]{:S(2)}, u32[]{:S(2)}) collective-permute-start(f32[75,1,128]{2,1,0:T(1,128)S(1)} %get-tuple-element.1975), channel_id=1, source_target_pairs={{0,16},{16,32},{32,48},{48,64},{64,80},{80,96},{96,112},{1,17},{17... | collective-permute-start | bytes 115208 | tf_op jit(solution)/shard_map/ppermute | solution.py:17
  245.0 2.2 collective-permute-done.20
  247.2 3.1 collective-permute-done.21
  252.0 2.6 fusion.129
  254.6 7.4 %all-to-all-start.2 = ((f32[16,128,4]{0,2,1:T(4,128)}), f32[16,128,4]{0,2,1:T(4,128)S(1)}, u32[]{:S(2)}, u32[]{:S(2)}) async-start(f32[16,128,4]{0,2,1:T(4,128)} %bitcast.32), calls=%async_computation.2 | async-start | bytes 524288 | tf_op jit(solution)/shard_map/all_to_all | solution.py:72
  262.0 14.7 %all-to-all-done.2 = f32[16,128,4]{0,2,1:T(4,128)S(1)} async-done(((f32[16,128,4]{0,2,1:T(4,128)}), f32[16,128,4]{0,2,1:T(4,128)S(1)}, u32[]{:S(2)}, u32[]{:S(2)}) %all-to-all-start.2) | async-done | bytes 32800 | tf_op jit(solution)/shard_map/all_to_all | solution.py:72
  277.4 7.7 %psum.30 = f32[4,128]{1,0:T(4,128)S(1)} all-reduce(f32[4,128]{1,0:T(4,128)S(1)} %reshape.212), channel_id=1, replica_groups=mesh['sec'=4,'lat'=8,'lon'=16] {'sec'}, use_global_device_ids=true, to_apply=%region_26.28 | all-reduce | flops 512 | bytes 4096 | tf_op jit(solution)/shard_map/psum | solution.py:88
  285.2 3.2 while.288
  288.4 2.7 while.289
  293.2 5.2 %collective-permute-start.27 = (f32[75,1,128]{2,1,0:T(1,128)}, f32[75,1,128]{2,1,0:T(1,128)}, u32[]{:S(2)}, u32[]{:S(2)}) collective-permute-start(f32[75,1,128]{2,1,0:T(1,128)} %get-tuple-element.1969), channel_id=1, source_target_pairs={{0,16},{16,32},{32,48},{48,64},{64,80},{80,96},{96,112},{1,17},{17... | collective-permute-start | bytes 115208 | tf_op jit(solution)/shard_map/ppermute | solution.py:17
  299.7 2.5 collective-permute-done.24
  302.3 3.0 collective-permute-done.25
  305.9 1.3 fusion.43
  307.3 3.0 while.290
  310.4 2.7 while.291
  313.2 1.3 collective-permute-start.30
  314.5 4.5 %collective-permute-start.31 = (f32[75,1,128]{2,1,0:T(1,128)S(1)}, f32[75,1,128]{2,1,0:T(1,128)S(1)}, u32[]{:S(2)}, u32[]{:S(2)}) collective-permute-start(f32[75,1,128]{2,1,0:T(1,128)S(1)} %get-tuple-element.1963), channel_id=1, source_target_pairs={{0,16},{16,32},{32,48},{48,64},{64,80},{80,96},{96,112},{1,17},{17... | collective-permute-start | bytes 115208 | tf_op jit(solution)/shard_map/ppermute | solution.py:17
  319.8 2.2 collective-permute-done.28
  322.0 3.1 collective-permute-done.29
  326.8 2.6 fusion.130
  329.4 7.4 %all-to-all-start.3 = ((f32[16,128,4]{0,2,1:T(4,128)}), f32[16,128,4]{0,2,1:T(4,128)S(1)}, u32[]{:S(2)}, u32[]{:S(2)}) async-start(f32[16,128,4]{0,2,1:T(4,128)} %bitcast.42), calls=%async_computation.3 | async-start | bytes 524288 | tf_op jit(solution)/shard_map/all_to_all | solution.py:72
  337.4 14.0 %all-to-all-done.3 = f32[16,128,4]{0,2,1:T(4,128)S(1)} async-done(((f32[16,128,4]{0,2,1:T(4,128)}), f32[16,128,4]{0,2,1:T(4,128)S(1)}, u32[]{:S(2)}, u32[]{:S(2)}) %all-to-all-start.3) | async-done | bytes 32800 | tf_op jit(solution)/shard_map/all_to_all | solution.py:72
  352.1 9.7 %psum.31 = f32[4,128]{1,0:T(4,128)S(1)} all-reduce(f32[4,128]{1,0:T(4,128)S(1)} %reshape.216), channel_id=1, replica_groups=mesh['sec'=4,'lat'=8,'lon'=16] {'sec'}, use_global_device_ids=true, to_apply=%region_35.37 | all-reduce | flops 512 | bytes 4096 | tf_op jit(solution)/shard_map/psum | solution.py:88
  (1382 shorter events, 106.0 us)
Async XLA Ops:
  0.0 66.8 %copy-start.9 = (s32[1,1,1,128,4]{3,4,2,1,0:T(4,128)S(1)}, s32[1,1,1,128,4]{3,4,2,1,0:T(4,128)}, u32[]{:S(2)}) copy-start(s32[1,1,1,128,4]{3,4,2,1,0:T(4,128)} %param.57) | copy-start | bytes 6148
  0.0 67.1 %copy-start.6 = (s32[4,128]{1,0:T(4,128)S(1)}, s32[4,128]{1,0:T(4,128)}, u32[]{:S(2)}) copy-start(s32[4,128]{1,0:T(4,128)} %param.55) | copy-start | bytes 6148
  1.1 73.8 %copy-start = (bf16[1,75,4,128]{3,2,1,0:T(4,128)(2,1)S(1)}, bf16[1,75,4,128]{3,2,1,0:T(4,128)(2,1)}, u32[]{:S(2)}) copy-start(bf16[1,75,4,128]{3,2,1,0:T(4,128)(2,1)} %param.53) | copy-start | bytes 230404
  1.1 73.8 %copy-start.1 = (bf16[1,75,4,128]{3,2,1,0:T(4,128)(2,1)S(1)}, bf16[1,75,4,128]{3,2,1,0:T(4,128)(2,1)}, u32[]{:S(2)}) copy-start(bf16[1,75,4,128]{3,2,1,0:T(4,128)(2,1)} %param.54) | copy-start | bytes 230404
  57.4 27.3 %copy-start.2 = (bf16[1,1,1,16,16,512]{5,4,3,2,1,0:T(8,128)(2,1)S(1)}, bf16[1,1,1,16,16,512]{5,4,3,2,1,0:T(8,128)(2,1)}, u32[]{:S(2)}) copy-start(bf16[1,1,1,16,16,512]{5,4,3,2,1,0:T(8,128)(2,1)} %param.56) | copy-start | bytes 786436
  57.6 9.5 %collective-permute-start = (f32[75,4,1]{2,1,0:T(4,128)S(1)}, f32[75,4,1]{2,1,0:T(4,128)S(1)}, u32[]{:S(2)}, u32[]{:S(2)}) collective-permute-start(f32[75,4,1]{2,1,0:T(4,128)S(1)} %get-tuple-element.2000), channel_id=1, source_target_pairs={{1,0},{2,1},{3,2},{4,3},{5,4},{6,5},{7,6},{8,7},{9,8},{10,9},{11,1... | collective-permute-start | bytes 3608 | tf_op jit(solution)/shard_map/ppermute | solution.py:20
  60.5 6.6 %collective-permute-start.1 = (f32[75,4,1]{2,1,0:T(4,128)S(1)}, f32[75,4,1]{2,1,0:T(4,128)S(1)}, u32[]{:S(2)}, u32[]{:S(2)}) collective-permute-start(f32[75,4,1]{2,1,0:T(4,128)S(1)} %get-tuple-element.2001), channel_id=1, source_target_pairs={{0,1},{1,2},{2,3},{3,4},{4,5},{5,6},{6,7},{7,8},{8,9},{9,10},{10,1... | collective-permute-start | bytes 3608 | tf_op jit(solution)/shard_map/ppermute | solution.py:17
  60.6 6.6 %collective-permute-start.2 = (f32[75,1,128]{2,1,0:T(1,128)S(1)}, f32[75,1,128]{2,1,0:T(1,128)S(1)}, u32[]{:S(2)}, u32[]{:S(2)}) collective-permute-start(f32[75,1,128]{2,1,0:T(1,128)S(1)} %get-tuple-element.2004), channel_id=1, source_target_pairs={{16,0},{32,16},{48,32},{64,48},{80,64},{96,80},{112,96},{17,1},{33... | collective-permute-start | bytes 115208 | tf_op jit(solution)/shard_map/ppermute | solution.py:20
  61.9 6.5 %collective-permute-start.3 = (f32[75,1,128]{2,1,0:T(1,128)S(1)}, f32[75,1,128]{2,1,0:T(1,128)S(1)}, u32[]{:S(2)}, u32[]{:S(2)}) collective-permute-start(f32[75,1,128]{2,1,0:T(1,128)S(1)} %get-tuple-element.2005), channel_id=1, source_target_pairs={{0,16},{16,32},{32,48},{48,64},{64,80},{80,96},{96,112},{1,17},{17... | collective-permute-start | bytes 115208 | tf_op jit(solution)/shard_map/ppermute | solution.py:17
  67.1 22.3 %copy-start.7 = (pred[512]{0:T(512)(128)(4,1)}, pred[512]{0:T(512)(128)(4,1)S(1)}, u32[]{:S(2)}) copy-start(pred[512]{0:T(512)(128)(4,1)S(1)} %compare_and_fusion) | copy-start | bytes 1540
  75.8 11.1 %collective-permute-start.4 = (f32[75,4,1]{2,1,0:T(4,128)}, f32[75,4,1]{2,1,0:T(4,128)}, u32[]{:S(2)}, u32[]{:S(2)}) collective-permute-start(f32[75,4,1]{2,1,0:T(4,128)} %get-tuple-element.1994), channel_id=1, source_target_pairs={{1,0},{2,1},{3,2},{4,3},{5,4},{6,5},{7,6},{8,7},{9,8},{10,9},{11,1... | collective-permute-start | bytes 3608 | tf_op jit(solution)/shard_map/ppermute | solution.py:20
  77.9 9.0 %collective-permute-start.5 = (f32[75,4,1]{2,1,0:T(4,128)}, f32[75,4,1]{2,1,0:T(4,128)}, u32[]{:S(2)}, u32[]{:S(2)}) collective-permute-start(f32[75,4,1]{2,1,0:T(4,128)} %get-tuple-element.1995), channel_id=1, source_target_pairs={{0,1},{1,2},{2,3},{3,4},{4,5},{5,6},{6,7},{7,8},{8,9},{9,10},{10,1... | collective-permute-start | bytes 3608 | tf_op jit(solution)/shard_map/ppermute | solution.py:17
  78.6 8.3 %collective-permute-start.6 = (f32[75,1,128]{2,1,0:T(1,128)}, f32[75,1,128]{2,1,0:T(1,128)S(1)}, u32[]{:S(2)}, u32[]{:S(2)}) collective-permute-start(f32[75,1,128]{2,1,0:T(1,128)} %get-tuple-element.1998), channel_id=1, source_target_pairs={{16,0},{32,16},{48,32},{64,48},{80,64},{96,80},{112,96},{17,1},{33... | collective-permute-start | bytes 115208 | tf_op jit(solution)/shard_map/ppermute | solution.py:20
  79.8 7.0 %collective-permute-start.7 = (f32[75,1,128]{2,1,0:T(1,128)}, f32[75,1,128]{2,1,0:T(1,128)S(1)}, u32[]{:S(2)}, u32[]{:S(2)}) collective-permute-start(f32[75,1,128]{2,1,0:T(1,128)} %get-tuple-element.1999), channel_id=1, source_target_pairs={{0,16},{16,32},{32,48},{48,64},{64,80},{80,96},{96,112},{1,17},{17... | collective-permute-start | bytes 115208 | tf_op jit(solution)/shard_map/ppermute | solution.py:17
  89.4 19.7 %copy-start.11 = (s32[1,1,1,128]{3,2,1,0:T(1,128)S(1)}, s32[1,1,1,128]{3,2,1,0:T(1,128)}, u32[]{:S(2)}) copy-start(s32[1,1,1,128]{3,2,1,0:T(1,128)} %param.59) | copy-start | bytes 1540
  89.4 19.8 %copy-start.10 = (s32[1,1,1,128,4]{3,4,2,1,0:T(4,128)S(1)}, s32[1,1,1,128,4]{3,4,2,1,0:T(4,128)}, u32[]{:S(2)}) copy-start(s32[1,1,1,128,4]{3,4,2,1,0:T(4,128)} %param.58) | copy-start | bytes 6148
  92.1 31.6 %all-to-all-start = ((f32[16,128,4]{0,2,1:T(4,128)}), f32[16,128,4]{0,2,1:T(4,128)S(1)}, u32[]{:S(2)}, u32[]{:S(2)}) async-start(f32[16,128,4]{0,2,1:T(4,128)} %bitcast.13), calls=%async_computation | async-start | bytes 524288 | tf_op jit(solution)/shard_map/all_to_all | solution.py:72
  139.9 13.3 %collective-permute-start.10 = (f32[75,1,128]{2,1,0:T(1,128)}, f32[75,1,128]{2,1,0:T(1,128)}, u32[]{:S(2)}, u32[]{:S(2)}) collective-permute-start(f32[75,1,128]{2,1,0:T(1,128)} %get-tuple-element.1992), channel_id=1, source_target_pairs={{16,0},{32,16},{48,32},{64,48},{80,64},{96,80},{112,96},{17,1},{33... | collective-permute-start | bytes 115208 | tf_op jit(solution)/shard_map/ppermute | solution.py:20
  141.1 12.7 %collective-permute-start.11 = (f32[75,1,128]{2,1,0:T(1,128)}, f32[75,1,128]{2,1,0:T(1,128)}, u32[]{:S(2)}, u32[]{:S(2)}) collective-permute-start(f32[75,1,128]{2,1,0:T(1,128)} %get-tuple-element.1993), channel_id=1, source_target_pairs={{0,16},{16,32},{32,48},{48,64},{64,80},{80,96},{96,112},{1,17},{17... | collective-permute-start | bytes 115208 | tf_op jit(solution)/shard_map/ppermute | solution.py:17
  147.1 3.1 collective-permute-start.8
  147.1 6.1 %collective-permute-start.9 = (f32[75,4,1]{2,1,0:T(4,128)}, f32[75,4,1]{2,1,0:T(4,128)S(1)}, u32[]{:S(2)}, u32[]{:S(2)}) collective-permute-start(f32[75,4,1]{2,1,0:T(4,128)} %get-tuple-element.1989), channel_id=1, source_target_pairs={{0,1},{1,2},{2,3},{3,4},{4,5},{5,6},{6,7},{7,8},{8,9},{9,10},{10,1... | collective-permute-start | bytes 3608 | tf_op jit(solution)/shard_map/ppermute | solution.py:17
  153.2 0.7 copy-start.3
  161.1 13.7 %copy-start.8 = (pred[512]{0:T(512)(128)(4,1)S(1)}, pred[512]{0:T(512)(128)(4,1)}, u32[]{:S(2)}) copy-start(pred[512]{0:T(512)(128)(4,1)} %copy-done.7) | copy-start | bytes 1540
  161.2 12.1 %collective-permute-start.14 = (f32[75,1,128]{2,1,0:T(1,128)S(1)}, f32[75,1,128]{2,1,0:T(1,128)S(1)}, u32[]{:S(2)}, u32[]{:S(2)}) collective-permute-start(f32[75,1,128]{2,1,0:T(1,128)S(1)} %get-tuple-element.1986), channel_id=1, source_target_pairs={{16,0},{32,16},{48,32},{64,48},{80,64},{96,80},{112,96},{17,1},{33... | collective-permute-start | bytes 115208 | tf_op jit(solution)/shard_map/ppermute | solution.py:20
  162.5 10.8 %collective-permute-start.15 = (f32[75,1,128]{2,1,0:T(1,128)S(1)}, f32[75,1,128]{2,1,0:T(1,128)S(1)}, u32[]{:S(2)}, u32[]{:S(2)}) collective-permute-start(f32[75,1,128]{2,1,0:T(1,128)S(1)} %get-tuple-element.1987), channel_id=1, source_target_pairs={{0,16},{16,32},{32,48},{48,64},{64,80},{80,96},{96,112},{1,17},{17... | collective-permute-start | bytes 115208 | tf_op jit(solution)/shard_map/ppermute | solution.py:17
  167.3 2.8 collective-permute-start.12
  167.4 5.9 %collective-permute-start.13 = (f32[75,4,1]{2,1,0:T(4,128)S(1)}, f32[75,4,1]{2,1,0:T(4,128)S(1)}, u32[]{:S(2)}, u32[]{:S(2)}) collective-permute-start(f32[75,4,1]{2,1,0:T(4,128)S(1)} %get-tuple-element.1983), channel_id=1, source_target_pairs={{0,1},{1,2},{2,3},{3,4},{4,5},{5,6},{6,7},{7,8},{8,9},{9,10},{10,1... | collective-permute-start | bytes 3608 | tf_op jit(solution)/shard_map/ppermute | solution.py:17
  177.5 22.1 %all-to-all-start.1 = ((f32[16,128,4]{0,2,1:T(4,128)}), f32[16,128,4]{0,2,1:T(4,128)S(1)}, u32[]{:S(2)}, u32[]{:S(2)}) async-start(f32[16,128,4]{0,2,1:T(4,128)} %bitcast.23), calls=%async_computation.1 | async-start | bytes 524288 | tf_op jit(solution)/shard_map/all_to_all | solution.py:72
  217.2 13.3 %collective-permute-start.18 = (f32[75,1,128]{2,1,0:T(1,128)}, f32[75,1,128]{2,1,0:T(1,128)}, u32[]{:S(2)}, u32[]{:S(2)}) collective-permute-start(f32[75,1,128]{2,1,0:T(1,128)} %get-tuple-element.1980), channel_id=1, source_target_pairs={{16,0},{32,16},{48,32},{64,48},{80,64},{96,80},{112,96},{17,1},{33... | collective-permute-start | bytes 115208 | tf_op jit(solution)/shard_map/ppermute | solution.py:20
  218.5 12.7 %collective-permute-start.19 = (f32[75,1,128]{2,1,0:T(1,128)}, f32[75,1,128]{2,1,0:T(1,128)}, u32[]{:S(2)}, u32[]{:S(2)}) collective-permute-start(f32[75,1,128]{2,1,0:T(1,128)} %get-tuple-element.1981), channel_id=1, source_target_pairs={{0,16},{16,32},{32,48},{48,64},{64,80},{80,96},{96,112},{1,17},{17... | collective-permute-start | bytes 115208 | tf_op jit(solution)/shard_map/ppermute | solution.py:17
  224.5 3.1 collective-permute-start.16
  224.5 6.1 %collective-permute-start.17 = (f32[75,4,1]{2,1,0:T(4,128)}, f32[75,4,1]{2,1,0:T(4,128)S(1)}, u32[]{:S(2)}, u32[]{:S(2)}) collective-permute-start(f32[75,4,1]{2,1,0:T(4,128)} %get-tuple-element.1977), channel_id=1, source_target_pairs={{0,1},{1,2},{2,3},{3,4},{4,5},{5,6},{6,7},{7,8},{8,9},{9,10},{10,1... | collective-permute-start | bytes 3608 | tf_op jit(solution)/shard_map/ppermute | solution.py:17
  230.5 0.7 copy-start.4
  238.5 11.9 %collective-permute-start.22 = (f32[75,1,128]{2,1,0:T(1,128)S(1)}, f32[75,1,128]{2,1,0:T(1,128)S(1)}, u32[]{:S(2)}, u32[]{:S(2)}) collective-permute-start(f32[75,1,128]{2,1,0:T(1,128)S(1)} %get-tuple-element.1974), channel_id=1, source_target_pairs={{16,0},{32,16},{48,32},{64,48},{80,64},{96,80},{112,96},{17,1},{33... | collective-permute-start | bytes 115208 | tf_op jit(solution)/shard_map/ppermute | solution.py:20
  239.8 10.6 %collective-permute-start.23 = (f32[75,1,128]{2,1,0:T(1,128)S(1)}, f32[75,1,128]{2,1,0:T(1,128)S(1)}, u32[]{:S(2)}, u32[]{:S(2)}) collective-permute-start(f32[75,1,128]{2,1,0:T(1,128)S(1)} %get-tuple-element.1975), channel_id=1, source_target_pairs={{0,16},{16,32},{32,48},{48,64},{64,80},{80,96},{96,112},{1,17},{17... | collective-permute-start | bytes 115208 | tf_op jit(solution)/shard_map/ppermute | solution.py:17
  244.5 2.8 collective-permute-start.20
  244.5 5.9 %collective-permute-start.21 = (f32[75,4,1]{2,1,0:T(4,128)S(1)}, f32[75,4,1]{2,1,0:T(4,128)S(1)}, u32[]{:S(2)}, u32[]{:S(2)}) collective-permute-start(f32[75,4,1]{2,1,0:T(4,128)S(1)} %get-tuple-element.1971), channel_id=1, source_target_pairs={{0,1},{1,2},{2,3},{3,4},{4,5},{5,6},{6,7},{7,8},{8,9},{9,10},{10,1... | collective-permute-start | bytes 3608 | tf_op jit(solution)/shard_map/ppermute | solution.py:17
  254.6 22.1 %all-to-all-start.2 = ((f32[16,128,4]{0,2,1:T(4,128)}), f32[16,128,4]{0,2,1:T(4,128)S(1)}, u32[]{:S(2)}, u32[]{:S(2)}) async-start(f32[16,128,4]{0,2,1:T(4,128)} %bitcast.32), calls=%async_computation.2 | async-start | bytes 524288 | tf_op jit(solution)/shard_map/all_to_all | solution.py:72
  291.9 13.3 %collective-permute-start.26 = (f32[75,1,128]{2,1,0:T(1,128)}, f32[75,1,128]{2,1,0:T(1,128)}, u32[]{:S(2)}, u32[]{:S(2)}) collective-permute-start(f32[75,1,128]{2,1,0:T(1,128)} %get-tuple-element.1968), channel_id=1, source_target_pairs={{16,0},{32,16},{48,32},{64,48},{80,64},{96,80},{112,96},{17,1},{33... | collective-permute-start | bytes 115208 | tf_op jit(solution)/shard_map/ppermute | solution.py:20
  293.2 12.7 %collective-permute-start.27 = (f32[75,1,128]{2,1,0:T(1,128)}, f32[75,1,128]{2,1,0:T(1,128)}, u32[]{:S(2)}, u32[]{:S(2)}) collective-permute-start(f32[75,1,128]{2,1,0:T(1,128)} %get-tuple-element.1969), channel_id=1, source_target_pairs={{0,16},{16,32},{32,48},{48,64},{64,80},{80,96},{96,112},{1,17},{17... | collective-permute-start | bytes 115208 | tf_op jit(solution)/shard_map/ppermute | solution.py:17
  299.2 3.1 collective-permute-start.24
  299.2 6.1 %collective-permute-start.25 = (f32[75,4,1]{2,1,0:T(4,128)}, f32[75,4,1]{2,1,0:T(4,128)S(1)}, u32[]{:S(2)}, u32[]{:S(2)}) collective-permute-start(f32[75,4,1]{2,1,0:T(4,128)} %get-tuple-element.1965), channel_id=1, source_target_pairs={{0,1},{1,2},{2,3},{3,4},{4,5},{5,6},{6,7},{7,8},{8,9},{9,10},{10,1... | collective-permute-start | bytes 3608 | tf_op jit(solution)/shard_map/ppermute | solution.py:17
  305.3 0.7 copy-start.5
  313.2 11.9 %collective-permute-start.30 = (f32[75,1,128]{2,1,0:T(1,128)S(1)}, f32[75,1,128]{2,1,0:T(1,128)S(1)}, u32[]{:S(2)}, u32[]{:S(2)}) collective-permute-start(f32[75,1,128]{2,1,0:T(1,128)S(1)} %get-tuple-element.1962), channel_id=1, source_target_pairs={{16,0},{32,16},{48,32},{64,48},{80,64},{96,80},{112,96},{17,1},{33... | collective-permute-start | bytes 115208 | tf_op jit(solution)/shard_map/ppermute | solution.py:20
  314.5 10.6 %collective-permute-start.31 = (f32[75,1,128]{2,1,0:T(1,128)S(1)}, f32[75,1,128]{2,1,0:T(1,128)S(1)}, u32[]{:S(2)}, u32[]{:S(2)}) collective-permute-start(f32[75,1,128]{2,1,0:T(1,128)S(1)} %get-tuple-element.1963), channel_id=1, source_target_pairs={{0,16},{16,32},{32,48},{48,64},{64,80},{80,96},{96,112},{1,17},{17... | collective-permute-start | bytes 115208 | tf_op jit(solution)/shard_map/ppermute | solution.py:17
  319.2 2.8 collective-permute-start.28
  319.3 5.9 %collective-permute-start.29 = (f32[75,4,1]{2,1,0:T(4,128)S(1)}, f32[75,4,1]{2,1,0:T(4,128)S(1)}, u32[]{:S(2)}, u32[]{:S(2)}) collective-permute-start(f32[75,4,1]{2,1,0:T(4,128)S(1)} %get-tuple-element.1959), channel_id=1, source_target_pairs={{0,1},{1,2},{2,3},{3,4},{4,5},{5,6},{6,7},{7,8},{8,9},{9,10},{10,1... | collective-permute-start | bytes 3608 | tf_op jit(solution)/shard_map/ppermute | solution.py:17
  329.4 22.1 %all-to-all-start.3 = ((f32[16,128,4]{0,2,1:T(4,128)}), f32[16,128,4]{0,2,1:T(4,128)S(1)}, u32[]{:S(2)}, u32[]{:S(2)}) async-start(f32[16,128,4]{0,2,1:T(4,128)} %bitcast.42), calls=%async_computation.3 | async-start | bytes 524288 | tf_op jit(solution)/shard_map/all_to_all | solution.py:72
where the time goes:
time: 365 us; the launch traced here: 362 us
  starting transfers between devices  96.5 us (26%)
  waiting for transfers between devices  91.7 us (25%)
  other arithmetic  85.1 us (23%)
  blocking collectives  36.2 us (10%)
  loops' own time  21.6 us (6%)
  local copies, waits for them, and re-layouts  17.9 us (5%)
  matrix products  12.5 us (3%)
    dynamic_update_slice x1200, other arithmetic, column_solve(): lax.scan(sweep_down, start_pair, (centre, lower_band, upper_band, right))  74.6 us
    all_to_all x4, waiting for transfers between devices, couple(): lax.all_to_all(contribution.reshape(block_cells, peer_count, capacity), (...  57.7 us
    ppermute x16, starting transfers between devices, extended(): lax.ppermute(lax.slice_in_dim(block, block.shape[dim] - width, None, axis...  42.1 us
    all_to_all x4, starting transfers between devices, couple(): lax.all_to_all(contribution.reshape(block_cells, peer_count, capacity), (...  39 us
    psum x4, blocking collectives, couple(): summed = lax.psum(accumulated * air_factor, 'sec')  36.2 us
    ppermute x16, waiting for transfers between devices, extended(): lax.ppermute(lax.slice_in_dim(block, block.shape[dim] - width, None, axis...  19.7 us
    ppermute x16, starting transfers between devices, extended(): lax.ppermute(lax.slice_in_dim(block, 0, width, axis=dim), axis, backward)  15.4 us
    ppermute x16, waiting for transfers between devices, extended(): lax.ppermute(lax.slice_in_dim(block, 0, width, axis=dim), axis, backward)  14.3 us
  transfers between devices with their start and end apart: 36, of which 17 were waited for; matrix products, arithmetic and copies ran while one was open for 2% of the time, Pallas kernels for 0%

commit v1 on v0

--- a/solution.py
+++ b/solution.py
@@ -85,7 +85,7 @@
     accumulated = jnp.dot(
         arrived, one_hot, precision=lax.Precision.HIGHEST, preferred_element_type=jnp.float32
     )
-    summed = lax.psum(accumulated * air_factor, "sec")
+    summed = jnp.sum(lax.all_gather(accumulated * air_factor, "sec"), axis=0)
     return summed.T.reshape(field_part.shape[1], field_part.shape[2])
 
 

time: 365 us -> 377 us (1.033)
  blocking collectives: 36.2 us -> 47.8 us
    all_gather x0 -> x4, blocking collectives: none -> 47.8 us  [couple(): summed = jnp.sum(lax.all_gather(accumulated * air_factor, 'sec'), axis=0)]
    psum x4 -> x0, blocking collectives: 36.2 us -> none  [couple(): summed = lax.psum(accumulated * air_factor, 'sec')]
where the time goes in v1:
time: 377 us; the launch traced here: 374 us
  starting transfers between devices  96.7 us (26%)
  waiting for transfers between devices  91.7 us (24%)
  other arithmetic  85.1 us (23%)
  blocking collectives  47.8 us (13%)
  loops' own time  21.6 us (6%)
  local copies, waits for them, and re-layouts  17.8 us (5%)
  matrix products  12.5 us (3%)
    dynamic_update_slice x1200, other arithmetic, column_solve(): lax.scan(sweep_down, start_pair, (centre, lower_band, upper_band, right))  74.6 us
    all_to_all x4, waiting for transfers between devices, couple(): lax.all_to_all(contribution.reshape(block_cells, peer_count, capacity), (...  57.7 us
    all_gather x4, blocking collectives, couple(): summed = jnp.sum(lax.all_gather(accumulated * air_factor, 'sec'), axis=0)  47.8 us
    ppermute x16, starting transfers between devices, extended(): lax.ppermute(lax.slice_in_dim(block, block.shape[dim] - width, None, axis...  42.4 us
    all_to_all x4, starting transfers between devices, couple(): lax.all_to_all(contribution.reshape(block_cells, peer_count, capacity), (...  39 us
    ppermute x16, waiting for transfers between devices, extended(): lax.ppermute(lax.slice_in_dim(block, block.shape[dim] - width, None, axis...  19.7 us
    ppermute x16, starting transfers between devices, extended(): lax.ppermute(lax.slice_in_dim(block, 0, width, axis=dim), axis, backward)  15.4 us
    ppermute x16, waiting for transfers between devices, extended(): lax.ppermute(lax.slice_in_dim(block, 0, width, axis=dim), axis, backward)  14.3 us
  transfers between devices with their start and end apart: 36, of which 17 were waited for; matrix products, arithmetic and copies ran while one was open for 2% of the time, Pallas kernels for 0%

profile of v1, /device:TPU:2, one launch (start us, length us, event | category | flops | bytes accessed | tf_op | source)
XLA Modules:
  0.0 374.3 jit_solution(11030811064749934293)
XLA Ops:
  1.1 52.6 %while.276 = (s32[]{:T(128)}, f32[4,128]{1,0:T(4,128)S(1)}, f32[4,128]{1,0:T(4,128)S(1)}, f32[75,4,128]{2,1,0:T(4,128)S(1)}, f32[75,4,128]{2,1,0:T(4,128)S(1)}, ...) while((s32[]{:T(128)}, f32[4,128]{1,0:T(4,128)S(1)}, ...), condition=%wide.region_1.2_spmd.clone, body=%wide.region_0.1_spmd.clone.sunk | while | flops 4611 | bytes 20603 | solution.py:40
  53.7 2.7 while.277
  57.6 2.9 collective-permute-start
  60.6 1.3 collective-permute-start.2
  61.9 4.9 %collective-permute-start.3 = (f32[75,1,128]{2,1,0:T(1,128)S(1)}, f32[75,1,128]{2,1,0:T(1,128)S(1)}, u32[]{:S(2)}, u32[]{:S(2)}) collective-permute-start(f32[75,1,128]{2,1,0:T(1,128)S(1)} %get-tuple-element.2005), channel_id=1, source_target_pairs={{0,16},{16,32},{32,48},{48,64},{64,80},{80,96},{96,112},{1,17},{17... | collective-permute-start | bytes 115208 | tf_op jit(solution)/shard_map/ppermute | solution.py:17
  68.9 3.2 while.278
  72.1 2.7 while.279
  75.8 2.1 collective-permute-start.4
  78.6 1.3 collective-permute-start.6
  79.8 4.9 %collective-permute-start.7 = (f32[75,1,128]{2,1,0:T(1,128)}, f32[75,1,128]{2,1,0:T(1,128)S(1)}, u32[]{:S(2)}, u32[]{:S(2)}) collective-permute-start(f32[75,1,128]{2,1,0:T(1,128)} %get-tuple-element.1999), channel_id=1, source_target_pairs={{0,16},{16,32},{32,48},{48,64},{64,80},{80,96},{96,112},{1,17},{17... | collective-permute-start | bytes 115208 | tf_op jit(solution)/shard_map/ppermute | solution.py:17
  84.8 2.1 copy.19
  86.9 1.3 fusion.69
  89.5 2.6 fusion.123
  92.1 16.9 %all-to-all-start = ((f32[16,128,4]{0,2,1:T(4,128)}), f32[16,128,4]{0,2,1:T(4,128)S(1)}, u32[]{:S(2)}, u32[]{:S(2)}) async-start(f32[16,128,4]{0,2,1:T(4,128)} %bitcast.13), calls=%async_computation | async-start | bytes 524288 | tf_op jit(solution)/shard_map/all_to_all | solution.py:72
  109.5 14.2 %all-to-all-done = f32[16,128,4]{0,2,1:T(4,128)S(1)} async-done(((f32[16,128,4]{0,2,1:T(4,128)}), f32[16,128,4]{0,2,1:T(4,128)S(1)}, u32[]{:S(2)}, u32[]{:S(2)}) %all-to-all-start) | async-done | bytes 32800 | tf_op jit(solution)/shard_map/all_to_all | solution.py:72
  124.3 12.0 %all-gather = f32[64,32]{1,0:T(8,128)S(1)} all-gather(f32[16,32]{1,0:T(8,128)S(1)} %convolution_multiply_fusion.3), channel_id=2, replica_groups=mesh['sec'=4,'lat'=8,'lon'=16] {'sec'}, dimensions={0}, use_global_device_ids=true | all-gather | bytes 10240 | tf_op jit(solution)/shard_map/all_gather | solution.py:88
  136.5 3.2 while.280
  139.7 2.7 while.281
  144.5 5.2 %collective-permute-start.11 = (f32[75,1,128]{2,1,0:T(1,128)}, f32[75,1,128]{2,1,0:T(1,128)}, u32[]{:S(2)}, u32[]{:S(2)}) collective-permute-start(f32[75,1,128]{2,1,0:T(1,128)} %get-tuple-element.1993), channel_id=1, source_target_pairs={{0,16},{16,32},{32,48},{48,64},{64,80},{80,96},{96,112},{1,17},{17... | collective-permute-start | bytes 115208 | tf_op jit(solution)/shard_map/ppermute | solution.py:17
  151.0 2.5 collective-permute-done.8
  153.6 3.0 collective-permute-done.9
  157.2 1.3 fusion.63
  158.6 3.0 while.282
  161.7 2.7 while.283
  164.5 1.3 collective-permute-start.14
  165.8 4.7 %collective-permute-start.15 = (f32[75,1,128]{2,1,0:T(1,128)S(1)}, f32[75,1,128]{2,1,0:T(1,128)S(1)}, u32[]{:S(2)}, u32[]{:S(2)}) collective-permute-start(f32[75,1,128]{2,1,0:T(1,128)S(1)} %get-tuple-element.1987), channel_id=1, source_target_pairs={{0,16},{16,32},{32,48},{48,64},{64,80},{80,96},{96,112},{1,17},{17... | collective-permute-start | bytes 115208 | tf_op jit(solution)/shard_map/ppermute | solution.py:17
  171.3 2.2 collective-permute-done.12
  173.5 3.1 collective-permute-done.13
  178.3 2.6 fusion.124
  180.9 7.4 %all-to-all-start.1 = ((f32[16,128,4]{0,2,1:T(4,128)}), f32[16,128,4]{0,2,1:T(4,128)S(1)}, u32[]{:S(2)}, u32[]{:S(2)}) async-start(f32[16,128,4]{0,2,1:T(4,128)} %bitcast.24), calls=%async_computation.1 | async-start | bytes 524288 | tf_op jit(solution)/shard_map/all_to_all | solution.py:72
  188.3 14.7 %all-to-all-done.1 = f32[16,128,4]{0,2,1:T(4,128)S(1)} async-done(((f32[16,128,4]{0,2,1:T(4,128)}), f32[16,128,4]{0,2,1:T(4,128)S(1)}, u32[]{:S(2)}, u32[]{:S(2)}) %all-to-all-start.1) | async-done | bytes 32800 | tf_op jit(solution)/shard_map/all_to_all | solution.py:72
  203.5 11.9 %all-gather.1 = f32[64,32]{1,0:T(8,128)S(1)} all-gather(f32[16,32]{1,0:T(8,128)S(1)} %convolution_multiply_fusion.2), channel_id=3, replica_groups=mesh['sec'=4,'lat'=8,'lon'=16] {'sec'}, dimensions={0}, use_global_device_ids=true | all-gather | bytes 10240 | tf_op jit(solution)/shard_map/all_gather | solution.py:88
  215.7 3.2 while.284
  218.9 2.7 while.285
  223.7 5.2 %collective-permute-start.19 = (f32[75,1,128]{2,1,0:T(1,128)}, f32[75,1,128]{2,1,0:T(1,128)}, u32[]{:S(2)}, u32[]{:S(2)}) collective-permute-start(f32[75,1,128]{2,1,0:T(1,128)} %get-tuple-element.1981), channel_id=1, source_target_pairs={{0,16},{16,32},{32,48},{48,64},{64,80},{80,96},{96,112},{1,17},{17... | collective-permute-start | bytes 115208 | tf_op jit(solution)/shard_map/ppermute | solution.py:17
  230.2 2.5 collective-permute-done.16
  232.7 3.0 collective-permute-done.17
  236.4 1.3 fusion.51
  237.7 3.0 while.286
  240.8 2.7 while.287
  243.7 1.3 collective-permute-start.22
  245.0 4.5 %collective-permute-start.23 = (f32[75,1,128]{2,1,0:T(1,128)S(1)}, f32[75,1,128]{2,1,0:T(1,128)S(1)}, u32[]{:S(2)}, u32[]{:S(2)}) collective-permute-start(f32[75,1,128]{2,1,0:T(1,128)S(1)} %get-tuple-element.1975), channel_id=1, source_target_pairs={{0,16},{16,32},{32,48},{48,64},{64,80},{80,96},{96,112},{1,17},{17... | collective-permute-start | bytes 115208 | tf_op jit(solution)/shard_map/ppermute | solution.py:17
  250.2 2.2 collective-permute-done.20
  252.5 3.1 collective-permute-done.21
  257.2 2.6 fusion.125
  259.8 7.4 %all-to-all-start.2 = ((f32[16,128,4]{0,2,1:T(4,128)}), f32[16,128,4]{0,2,1:T(4,128)S(1)}, u32[]{:S(2)}, u32[]{:S(2)}) async-start(f32[16,128,4]{0,2,1:T(4,128)} %bitcast.34), calls=%async_computation.2 | async-start | bytes 524288 | tf_op jit(solution)/shard_map/all_to_all | solution.py:72
  267.2 14.7 %all-to-all-done.2 = f32[16,128,4]{0,2,1:T(4,128)S(1)} async-done(((f32[16,128,4]{0,2,1:T(4,128)}), f32[16,128,4]{0,2,1:T(4,128)S(1)}, u32[]{:S(2)}, u32[]{:S(2)}) %all-to-all-start.2) | async-done | bytes 32800 | tf_op jit(solution)/shard_map/all_to_all | solution.py:72
  282.4 11.9 %all-gather.2 = f32[64,32]{1,0:T(8,128)S(1)} all-gather(f32[16,32]{1,0:T(8,128)S(1)} %convolution_multiply_fusion.1), channel_id=4, replica_groups=mesh['sec'=4,'lat'=8,'lon'=16] {'sec'}, dimensions={0}, use_global_device_ids=true | all-gather | bytes 10240 | tf_op jit(solution)/shard_map/all_gather | solution.py:88
  294.6 3.2 while.288
  297.8 2.7 while.289
  302.6 5.4 %collective-permute-start.27 = (f32[75,1,128]{2,1,0:T(1,128)}, f32[75,1,128]{2,1,0:T(1,128)}, u32[]{:S(2)}, u32[]{:S(2)}) collective-permute-start(f32[75,1,128]{2,1,0:T(1,128)} %get-tuple-element.1969), channel_id=1, source_target_pairs={{0,16},{16,32},{32,48},{48,64},{64,80},{80,96},{96,112},{1,17},{17... | collective-permute-start | bytes 115208 | tf_op jit(solution)/shard_map/ppermute | solution.py:17
  309.3 2.5 collective-permute-done.24
  311.9 3.0 collective-permute-done.25
  315.6 1.3 fusion.39
  316.9 3.0 while.290
  320.0 2.7 while.291
  322.9 1.3 collective-permute-start.30
  324.2 4.5 %collective-permute-start.31 = (f32[75,1,128]{2,1,0:T(1,128)S(1)}, f32[75,1,128]{2,1,0:T(1,128)S(1)}, u32[]{:S(2)}, u32[]{:S(2)}) collective-permute-start(f32[75,1,128]{2,1,0:T(1,128)S(1)} %get-tuple-element.1963), channel_id=1, source_target_pairs={{0,16},{16,32},{32,48},{48,64},{64,80},{80,96},{96,112},{1,17},{17... | collective-permute-start | bytes 115208 | tf_op jit(solution)/shard_map/ppermute | solution.py:17
  329.4 2.2 collective-permute-done.28
  331.6 3.1 collective-permute-done.29
  336.4 2.6 fusion.126
  339.0 7.4 %all-to-all-start.3 = ((f32[16,128,4]{0,2,1:T(4,128)}), f32[16,128,4]{0,2,1:T(4,128)S(1)}, u32[]{:S(2)}, u32[]{:S(2)}) async-start(f32[16,128,4]{0,2,1:T(4,128)} %bitcast.45), calls=%async_computation.3 | async-start | bytes 524288 | tf_op jit(solution)/shard_map/all_to_all | solution.py:72
  347.0 14.0 %all-to-all-done.3 = f32[16,128,4]{0,2,1:T(4,128)S(1)} async-done(((f32[16,128,4]{0,2,1:T(4,128)}), f32[16,128,4]{0,2,1:T(4,128)S(1)}, u32[]{:S(2)}, u32[]{:S(2)}) %all-to-all-start.3) | async-done | bytes 32800 | tf_op jit(solution)/shard_map/all_to_all | solution.py:72
  361.6 11.9 %all-gather.3 = f32[64,32]{1,0:T(8,128)S(1)} all-gather(f32[16,32]{1,0:T(8,128)S(1)} %convolution_multiply_fusion), channel_id=5, replica_groups=mesh['sec'=4,'lat'=8,'lon'=16] {'sec'}, dimensions={0}, use_global_device_ids=true | all-gather | bytes 10240 | tf_op jit(solution)/shard_map/all_gather | solution.py:88
  (1386 shorter events, 106.0 us)
Async XLA Ops:
  0.0 66.8 %copy-start.9 = (s32[1,1,1,128,4]{3,4,2,1,0:T(4,128)S(1)}, s32[1,1,1,128,4]{3,4,2,1,0:T(4,128)}, u32[]{:S(2)}) copy-start(s32[1,1,1,128,4]{3,4,2,1,0:T(4,128)} %param.57) | copy-start | bytes 6148
  0.0 67.1 %copy-start.6 = (s32[4,128]{1,0:T(4,128)S(1)}, s32[4,128]{1,0:T(4,128)}, u32[]{:S(2)}) copy-start(s32[4,128]{1,0:T(4,128)} %param.55) | copy-start | bytes 6148
  1.1 73.8 %copy-start = (bf16[1,75,4,128]{3,2,1,0:T(4,128)(2,1)S(1)}, bf16[1,75,4,128]{3,2,1,0:T(4,128)(2,1)}, u32[]{:S(2)}) copy-start(bf16[1,75,4,128]{3,2,1,0:T(4,128)(2,1)} %param.53) | copy-start | bytes 230404
  1.1 73.8 %copy-start.1 = (bf16[1,75,4,128]{3,2,1,0:T(4,128)(2,1)S(1)}, bf16[1,75,4,128]{3,2,1,0:T(4,128)(2,1)}, u32[]{:S(2)}) copy-start(bf16[1,75,4,128]{3,2,1,0:T(4,128)(2,1)} %param.54) | copy-start | bytes 230404
  57.4 27.3 %copy-start.2 = (bf16[1,1,1,16,16,512]{5,4,3,2,1,0:T(8,128)(2,1)S(1)}, bf16[1,1,1,16,16,512]{5,4,3,2,1,0:T(8,128)(2,1)}, u32[]{:S(2)}) copy-start(bf16[1,1,1,16,16,512]{5,4,3,2,1,0:T(8,128)(2,1)} %param.56) | copy-start | bytes 786436
  57.6 9.5 %collective-permute-start = (f32[75,4,1]{2,1,0:T(4,128)S(1)}, f32[75,4,1]{2,1,0:T(4,128)S(1)}, u32[]{:S(2)}, u32[]{:S(2)}) collective-permute-start(f32[75,4,1]{2,1,0:T(4,128)S(1)} %get-tuple-element.2000), channel_id=1, source_target_pairs={{1,0},{2,1},{3,2},{4,3},{5,4},{6,5},{7,6},{8,7},{9,8},{10,9},{11,1... | collective-permute-start | bytes 3608 | tf_op jit(solution)/shard_map/ppermute | solution.py:20
  60.5 6.6 %collective-permute-start.1 = (f32[75,4,1]{2,1,0:T(4,128)S(1)}, f32[75,4,1]{2,1,0:T(4,128)S(1)}, u32[]{:S(2)}, u32[]{:S(2)}) collective-permute-start(f32[75,4,1]{2,1,0:T(4,128)S(1)} %get-tuple-element.2001), channel_id=1, source_target_pairs={{0,1},{1,2},{2,3},{3,4},{4,5},{5,6},{6,7},{7,8},{8,9},{9,10},{10,1... | collective-permute-start | bytes 3608 | tf_op jit(solution)/shard_map/ppermute | solution.py:17
  60.6 6.6 %collective-permute-start.2 = (f32[75,1,128]{2,1,0:T(1,128)S(1)}, f32[75,1,128]{2,1,0:T(1,128)S(1)}, u32[]{:S(2)}, u32[]{:S(2)}) collective-permute-start(f32[75,1,128]{2,1,0:T(1,128)S(1)} %get-tuple-element.2004), channel_id=1, source_target_pairs={{16,0},{32,16},{48,32},{64,48},{80,64},{96,80},{112,96},{17,1},{33... | collective-permute-start | bytes 115208 | tf_op jit(solution)/shard_map/ppermute | solution.py:20
  61.9 6.5 %collective-permute-start.3 = (f32[75,1,128]{2,1,0:T(1,128)S(1)}, f32[75,1,128]{2,1,0:T(1,128)S(1)}, u32[]{:S(2)}, u32[]{:S(2)}) collective-permute-start(f32[75,1,128]{2,1,0:T(1,128)S(1)} %get-tuple-element.2005), channel_id=1, source_target_pairs={{0,16},{16,32},{32,48},{48,64},{64,80},{80,96},{96,112},{1,17},{17... | collective-permute-start | bytes 115208 | tf_op jit(solution)/shard_map/ppermute | solution.py:17
  67.1 22.3 %copy-start.7 = (pred[512]{0:T(512)(128)(4,1)}, pred[512]{0:T(512)(128)(4,1)S(1)}, u32[]{:S(2)}) copy-start(pred[512]{0:T(512)(128)(4,1)S(1)} %compare_and_fusion) | copy-start | bytes 1540
  75.8 11.1 %collective-permute-start.4 = (f32[75,4,1]{2,1,0:T(4,128)}, f32[75,4,1]{2,1,0:T(4,128)}, u32[]{:S(2)}, u32[]{:S(2)}) collective-permute-start(f32[75,4,1]{2,1,0:T(4,128)} %get-tuple-element.1994), channel_id=1, source_target_pairs={{1,0},{2,1},{3,2},{4,3},{5,4},{6,5},{7,6},{8,7},{9,8},{10,9},{11,1... | collective-permute-start | bytes 3608 | tf_op jit(solution)/shard_map/ppermute | solution.py:20
  77.9 9.0 %collective-permute-start.5 = (f32[75,4,1]{2,1,0:T(4,128)}, f32[75,4,1]{2,1,0:T(4,128)}, u32[]{:S(2)}, u32[]{:S(2)}) collective-permute-start(f32[75,4,1]{2,1,0:T(4,128)} %get-tuple-element.1995), channel_id=1, source_target_pairs={{0,1},{1,2},{2,3},{3,4},{4,5},{5,6},{6,7},{7,8},{8,9},{9,10},{10,1... | collective-permute-start | bytes 3608 | tf_op jit(solution)/shard_map/ppermute | solution.py:17
  78.6 8.3 %collective-permute-start.6 = (f32[75,1,128]{2,1,0:T(1,128)}, f32[75,1,128]{2,1,0:T(1,128)S(1)}, u32[]{:S(2)}, u32[]{:S(2)}) collective-permute-start(f32[75,1,128]{2,1,0:T(1,128)} %get-tuple-element.1998), channel_id=1, source_target_pairs={{16,0},{32,16},{48,32},{64,48},{80,64},{96,80},{112,96},{17,1},{33... | collective-permute-start | bytes 115208 | tf_op jit(solution)/shard_map/ppermute | solution.py:20
  79.8 7.0 %collective-permute-start.7 = (f32[75,1,128]{2,1,0:T(1,128)}, f32[75,1,128]{2,1,0:T(1,128)S(1)}, u32[]{:S(2)}, u32[]{:S(2)}) collective-permute-start(f32[75,1,128]{2,1,0:T(1,128)} %get-tuple-element.1999), channel_id=1, source_target_pairs={{0,16},{16,32},{32,48},{48,64},{64,80},{80,96},{96,112},{1,17},{17... | collective-permute-start | bytes 115208 | tf_op jit(solution)/shard_map/ppermute | solution.py:17
  89.4 19.7 %copy-start.11 = (s32[1,1,1,128]{3,2,1,0:T(1,128)S(1)}, s32[1,1,1,128]{3,2,1,0:T(1,128)}, u32[]{:S(2)}) copy-start(s32[1,1,1,128]{3,2,1,0:T(1,128)} %param.59) | copy-start | bytes 1540
  89.4 19.8 %copy-start.10 = (s32[1,1,1,128,4]{3,4,2,1,0:T(4,128)S(1)}, s32[1,1,1,128,4]{3,4,2,1,0:T(4,128)}, u32[]{:S(2)}) copy-start(s32[1,1,1,128,4]{3,4,2,1,0:T(4,128)} %param.58) | copy-start | bytes 6148
  92.1 31.6 %all-to-all-start = ((f32[16,128,4]{0,2,1:T(4,128)}), f32[16,128,4]{0,2,1:T(4,128)S(1)}, u32[]{:S(2)}, u32[]{:S(2)}) async-start(f32[16,128,4]{0,2,1:T(4,128)} %bitcast.13), calls=%async_computation | async-start | bytes 524288 | tf_op jit(solution)/shard_map/all_to_all | solution.py:72
  143.2 13.3 %collective-permute-start.10 = (f32[75,1,128]{2,1,0:T(1,128)}, f32[75,1,128]{2,1,0:T(1,128)}, u32[]{:S(2)}, u32[]{:S(2)}) collective-permute-start(f32[75,1,128]{2,1,0:T(1,128)} %get-tuple-element.1992), channel_id=1, source_target_pairs={{16,0},{32,16},{48,32},{64,48},{80,64},{96,80},{112,96},{17,1},{33... | collective-permute-start | bytes 115208 | tf_op jit(solution)/shard_map/ppermute | solution.py:20
  144.5 12.7 %collective-permute-start.11 = (f32[75,1,128]{2,1,0:T(1,128)}, f32[75,1,128]{2,1,0:T(1,128)}, u32[]{:S(2)}, u32[]{:S(2)}) collective-permute-start(f32[75,1,128]{2,1,0:T(1,128)} %get-tuple-element.1993), channel_id=1, source_target_pairs={{0,16},{16,32},{32,48},{48,64},{64,80},{80,96},{96,112},{1,17},{17... | collective-permute-start | bytes 115208 | tf_op jit(solution)/shard_map/ppermute | solution.py:17
  150.5 3.1 collective-permute-start.8
  150.5 6.1 %collective-permute-start.9 = (f32[75,4,1]{2,1,0:T(4,128)}, f32[75,4,1]{2,1,0:T(4,128)S(1)}, u32[]{:S(2)}, u32[]{:S(2)}) collective-permute-start(f32[75,4,1]{2,1,0:T(4,128)} %get-tuple-element.1989), channel_id=1, source_target_pairs={{0,1},{1,2},{2,3},{3,4},{4,5},{5,6},{6,7},{7,8},{8,9},{9,10},{10,1... | collective-permute-start | bytes 3608 | tf_op jit(solution)/shard_map/ppermute | solution.py:17
  156.6 0.7 copy-start.3
  164.5 13.7 %copy-start.8 = (pred[512]{0:T(512)(128)(4,1)S(1)}, pred[512]{0:T(512)(128)(4,1)}, u32[]{:S(2)}) copy-start(pred[512]{0:T(512)(128)(4,1)} %copy-done.7) | copy-start | bytes 1540
  164.5 12.1 %collective-permute-start.14 = (f32[75,1,128]{2,1,0:T(1,128)S(1)}, f32[75,1,128]{2,1,0:T(1,128)S(1)}, u32[]{:S(2)}, u32[]{:S(2)}) collective-permute-start(f32[75,1,128]{2,1,0:T(1,128)S(1)} %get-tuple-element.1986), channel_id=1, source_target_pairs={{16,0},{32,16},{48,32},{64,48},{80,64},{96,80},{112,96},{17,1},{33... | collective-permute-start | bytes 115208 | tf_op jit(solution)/shard_map/ppermute | solution.py:20
  165.8 10.8 %collective-permute-start.15 = (f32[75,1,128]{2,1,0:T(1,128)S(1)}, f32[75,1,128]{2,1,0:T(1,128)S(1)}, u32[]{:S(2)}, u32[]{:S(2)}) collective-permute-start(f32[75,1,128]{2,1,0:T(1,128)S(1)} %get-tuple-element.1987), channel_id=1, source_target_pairs={{0,16},{16,32},{32,48},{48,64},{64,80},{80,96},{96,112},{1,17},{17... | collective-permute-start | bytes 115208 | tf_op jit(solution)/shard_map/ppermute | solution.py:17
  170.7 2.8 collective-permute-start.12
  170.8 5.9 %collective-permute-start.13 = (f32[75,4,1]{2,1,0:T(4,128)S(1)}, f32[75,4,1]{2,1,0:T(4,128)S(1)}, u32[]{:S(2)}, u32[]{:S(2)}) collective-permute-start(f32[75,4,1]{2,1,0:T(4,128)S(1)} %get-tuple-element.1983), channel_id=1, source_target_pairs={{0,1},{1,2},{2,3},{3,4},{4,5},{5,6},{6,7},{7,8},{8,9},{9,10},{10,1... | collective-permute-start | bytes 3608 | tf_op jit(solution)/shard_map/ppermute | solution.py:17
  180.9 22.1 %all-to-all-start.1 = ((f32[16,128,4]{0,2,1:T(4,128)}), f32[16,128,4]{0,2,1:T(4,128)S(1)}, u32[]{:S(2)}, u32[]{:S(2)}) async-start(f32[16,128,4]{0,2,1:T(4,128)} %bitcast.24), calls=%async_computation.1 | async-start | bytes 524288 | tf_op jit(solution)/shard_map/all_to_all | solution.py:72
  222.4 13.3 %collective-permute-start.18 = (f32[75,1,128]{2,1,0:T(1,128)}, f32[75,1,128]{2,1,0:T(1,128)}, u32[]{:S(2)}, u32[]{:S(2)}) collective-permute-start(f32[75,1,128]{2,1,0:T(1,128)} %get-tuple-element.1980), channel_id=1, source_target_pairs={{16,0},{32,16},{48,32},{64,48},{80,64},{96,80},{112,96},{17,1},{33... | collective-permute-start | bytes 115208 | tf_op jit(solution)/shard_map/ppermute | solution.py:20
  223.7 12.7 %collective-permute-start.19 = (f32[75,1,128]{2,1,0:T(1,128)}, f32[75,1,128]{2,1,0:T(1,128)}, u32[]{:S(2)}, u32[]{:S(2)}) collective-permute-start(f32[75,1,128]{2,1,0:T(1,128)} %get-tuple-element.1981), channel_id=1, source_target_pairs={{0,16},{16,32},{32,48},{48,64},{64,80},{80,96},{96,112},{1,17},{17... | collective-permute-start | bytes 115208 | tf_op jit(solution)/shard_map/ppermute | solution.py:17
  229.7 3.1 collective-permute-start.16
  229.7 6.1 %collective-permute-start.17 = (f32[75,4,1]{2,1,0:T(4,128)}, f32[75,4,1]{2,1,0:T(4,128)S(1)}, u32[]{:S(2)}, u32[]{:S(2)}) collective-permute-start(f32[75,4,1]{2,1,0:T(4,128)} %get-tuple-element.1977), channel_id=1, source_target_pairs={{0,1},{1,2},{2,3},{3,4},{4,5},{5,6},{6,7},{7,8},{8,9},{9,10},{10,1... | collective-permute-start | bytes 3608 | tf_op jit(solution)/shard_map/ppermute | solution.py:17
  235.7 0.7 copy-start.4
  243.7 11.9 %collective-permute-start.22 = (f32[75,1,128]{2,1,0:T(1,128)S(1)}, f32[75,1,128]{2,1,0:T(1,128)S(1)}, u32[]{:S(2)}, u32[]{:S(2)}) collective-permute-start(f32[75,1,128]{2,1,0:T(1,128)S(1)} %get-tuple-element.1974), channel_id=1, source_target_pairs={{16,0},{32,16},{48,32},{64,48},{80,64},{96,80},{112,96},{17,1},{33... | collective-permute-start | bytes 115208 | tf_op jit(solution)/shard_map/ppermute | solution.py:20
  245.0 10.6 %collective-permute-start.23 = (f32[75,1,128]{2,1,0:T(1,128)S(1)}, f32[75,1,128]{2,1,0:T(1,128)S(1)}, u32[]{:S(2)}, u32[]{:S(2)}) collective-permute-start(f32[75,1,128]{2,1,0:T(1,128)S(1)} %get-tuple-element.1975), channel_id=1, source_target_pairs={{0,16},{16,32},{32,48},{48,64},{64,80},{80,96},{96,112},{1,17},{17... | collective-permute-start | bytes 115208 | tf_op jit(solution)/shard_map/ppermute | solution.py:17
  249.7 2.8 collective-permute-start.20
  249.7 5.9 %collective-permute-start.21 = (f32[75,4,1]{2,1,0:T(4,128)S(1)}, f32[75,4,1]{2,1,0:T(4,128)S(1)}, u32[]{:S(2)}, u32[]{:S(2)}) collective-permute-start(f32[75,4,1]{2,1,0:T(4,128)S(1)} %get-tuple-element.1971), channel_id=1, source_target_pairs={{0,1},{1,2},{2,3},{3,4},{4,5},{5,6},{6,7},{7,8},{8,9},{9,10},{10,1... | collective-permute-start | bytes 3608 | tf_op jit(solution)/shard_map/ppermute | solution.py:17
  259.8 22.1 %all-to-all-start.2 = ((f32[16,128,4]{0,2,1:T(4,128)}), f32[16,128,4]{0,2,1:T(4,128)S(1)}, u32[]{:S(2)}, u32[]{:S(2)}) async-start(f32[16,128,4]{0,2,1:T(4,128)} %bitcast.34), calls=%async_computation.2 | async-start | bytes 524288 | tf_op jit(solution)/shard_map/all_to_all | solution.py:72
  301.4 13.5 %collective-permute-start.26 = (f32[75,1,128]{2,1,0:T(1,128)}, f32[75,1,128]{2,1,0:T(1,128)}, u32[]{:S(2)}, u32[]{:S(2)}) collective-permute-start(f32[75,1,128]{2,1,0:T(1,128)} %get-tuple-element.1968), channel_id=1, source_target_pairs={{16,0},{32,16},{48,32},{64,48},{80,64},{96,80},{112,96},{17,1},{33... | collective-permute-start | bytes 115208 | tf_op jit(solution)/shard_map/ppermute | solution.py:20
  302.6 12.9 %collective-permute-start.27 = (f32[75,1,128]{2,1,0:T(1,128)}, f32[75,1,128]{2,1,0:T(1,128)}, u32[]{:S(2)}, u32[]{:S(2)}) collective-permute-start(f32[75,1,128]{2,1,0:T(1,128)} %get-tuple-element.1969), channel_id=1, source_target_pairs={{0,16},{16,32},{32,48},{48,64},{64,80},{80,96},{96,112},{1,17},{17... | collective-permute-start | bytes 115208 | tf_op jit(solution)/shard_map/ppermute | solution.py:17
  308.8 3.1 collective-permute-start.24
  308.8 6.1 %collective-permute-start.25 = (f32[75,4,1]{2,1,0:T(4,128)}, f32[75,4,1]{2,1,0:T(4,128)S(1)}, u32[]{:S(2)}, u32[]{:S(2)}) collective-permute-start(f32[75,4,1]{2,1,0:T(4,128)} %get-tuple-element.1965), channel_id=1, source_target_pairs={{0,1},{1,2},{2,3},{3,4},{4,5},{5,6},{6,7},{7,8},{8,9},{9,10},{10,1... | collective-permute-start | bytes 3608 | tf_op jit(solution)/shard_map/ppermute | solution.py:17
  314.9 0.7 copy-start.5
  322.9 11.9 %collective-permute-start.30 = (f32[75,1,128]{2,1,0:T(1,128)S(1)}, f32[75,1,128]{2,1,0:T(1,128)S(1)}, u32[]{:S(2)}, u32[]{:S(2)}) collective-permute-start(f32[75,1,128]{2,1,0:T(1,128)S(1)} %get-tuple-element.1962), channel_id=1, source_target_pairs={{16,0},{32,16},{48,32},{64,48},{80,64},{96,80},{112,96},{17,1},{33... | collective-permute-start | bytes 115208 | tf_op jit(solution)/shard_map/ppermute | solution.py:20
  324.2 10.6 %collective-permute-start.31 = (f32[75,1,128]{2,1,0:T(1,128)S(1)}, f32[75,1,128]{2,1,0:T(1,128)S(1)}, u32[]{:S(2)}, u32[]{:S(2)}) collective-permute-start(f32[75,1,128]{2,1,0:T(1,128)S(1)} %get-tuple-element.1963), channel_id=1, source_target_pairs={{0,16},{16,32},{32,48},{48,64},{64,80},{80,96},{96,112},{1,17},{17... | collective-permute-start | bytes 115208 | tf_op jit(solution)/shard_map/ppermute | solution.py:17
  328.9 2.8 collective-permute-start.28
  328.9 5.9 %collective-permute-start.29 = (f32[75,4,1]{2,1,0:T(4,128)S(1)}, f32[75,4,1]{2,1,0:T(4,128)S(1)}, u32[]{:S(2)}, u32[]{:S(2)}) collective-permute-start(f32[75,4,1]{2,1,0:T(4,128)S(1)} %get-tuple-element.1959), channel_id=1, source_target_pairs={{0,1},{1,2},{2,3},{3,4},{4,5},{5,6},{6,7},{7,8},{8,9},{9,10},{10,1... | collective-permute-start | bytes 3608 | tf_op jit(solution)/shard_map/ppermute | solution.py:17
  339.0 22.1 %all-to-all-start.3 = ((f32[16,128,4]{0,2,1:T(4,128)}), f32[16,128,4]{0,2,1:T(4,128)S(1)}, u32[]{:S(2)}, u32[]{:S(2)}) async-start(f32[16,128,4]{0,2,1:T(4,128)} %bitcast.45), calls=%async_computation.3 | async-start | bytes 524288 | tf_op jit(solution)/shard_map/all_to_all | solution.py:72
